TPU v7x, 32 devices: a whole 2x2x4 slice. The times are simulated.
32 devices in a mesh: seq: 8 (over z, x), ch: 4 (over y, core).
Axes of the slice: x: 2, y: 2, z: 4, core: 2. Of those that a mesh axis runs over, the one named last changes fastest.
Arguments:
- tokens: int32 [2, 4096], P(None, 'seq'), may hold values from 0 to 3
- masked: int32 [2, 4096], P(None, 'seq'), may hold values 0 or 1
- hidden_forward: bfloat16 [2, 4096, 1024], P(None, 'seq', 'ch'), may hold values from -16 to 16
- hidden_reverse: bfloat16 [2, 4096, 1024], P(None, 'seq', 'ch'), may hold values from -16 to 16
- embed_table: bfloat16 [5, 1024], P(None, 'ch'), may hold values from -3 to 3
- conv_kernel: float32 [7, 1024], P(None, 'ch'), may hold values from -2.4 to 2.4
- conv_bias: float32 [1024], P('ch'), may hold values from -3 to 3
- norm_gain: float32 [1024], P('ch'), may hold values from 0.25 to 1.75
- w_gate: bfloat16 [1024, 4096], P(None, 'ch'), may hold values from -0.1875 to 0.1875
- w_value: bfloat16 [1024, 4096], P(None, 'ch'), may hold values from -0.1875 to 0.1875
- w_out: bfloat16 [4096, 1024], P('ch'), may hold values from -0.09375 to 0.09375
Outputs:
- out_forward: bfloat16 [2, 4096, 1024], P(None, 'seq', 'ch')
- out_reverse: bfloat16 [2, 4096, 1024], P(None, 'seq', 'ch')
Inputs may be any that keep to these rules, and one draw needn't show every extreme that they name: `tokens`: base ids A, C, G, T are 0, 1, 2, 3 and the complement of b is 3 - b.
All inputs are finite; a program needn't handle non-finite values. No bound on the sum of `masked` on one device may be relied on, other than what follows from the above.
Results may differ from a plain program's by a relative error of at most 0.0067.
Values may be sent and summed in bfloat16 or wider, within the bound.
No kernel may reach another device: no remote copies, remote signals or barrier semaphores. Data moves between devices by JAX's collectives and lax.ppermute only.
A program may use at most 128 MiB of HBM per device.

v0:
```python
import jax
import jax.numpy as jnp
from jax import lax
from jax.sharding import PartitionSpec as P


def mirror(value, axes, count):
    return lax.ppermute(value, axes, [(k, count - 1 - k) for k in range(count)])


def partner(value, axis, bit):
    mask = 1 << bit
    return lax.ppermute(value, axis, [(k, k ^ mask) for k in range(lax.axis_size(axis))])


def padded_2(cells, axis, dim, width):
    count = lax.axis_size(axis)
    ends = count - 1
    head = lax.slice_in_dim(cells, 0, width, axis=dim)
    tail = lax.slice_in_dim(cells, cells.shape[dim] - width, cells.shape[dim], axis=dim)
    return jnp.concatenate(
        [
            lax.ppermute(tail, axis, [(i, (i + 1) % count) for i in range(ends)]),
            cells,
            lax.ppermute(head, axis, [((i + 1) % count, i) for i in range(ends)]),
        ],
        axis=dim,
    )


def embedded(bases, table):
    out = jnp.zeros(bases.shape + (table.shape[1],), jnp.float32)
    for v in range(table.shape[0]):
        out = out + jnp.where(bases[..., None] == v, table[v], 0.0)
    return out


def gather_blocks(block, bits, me):
    cur = block[None]
    for bit in reversed(range(bits)):
        other = partner(cur, "ch", bit)
        low = me >> bit & 1 == 0
        first = jnp.where(low, cur, other)
        second = jnp.where(low, other, cur)
        cur = jnp.stack([first, second], axis=1).reshape((-1,) + block.shape)
    return cur


def scatter_blocks(part, bits, me):
    cur = part
    for bit in range(bits):
        cur = cur.reshape((-1, 2) + part.shape[1:])
        low = me >> bit & 1 == 0
        keep = jnp.where(low, cur[:, 0], cur[:, 1])
        give = jnp.where(low, cur[:, 1], cur[:, 0])
        if bit > 0:
            give = give.astype(jnp.bfloat16)
        cur = keep + partner(give, "ch", bit).astype(jnp.float32)
    return cur[0]


def local(
    tokens,
    masked,
    hidden_forward,
    hidden_reverse,
    embed_table,
    conv_kernel,
    conv_bias,
    norm_gain,
    w_gate,
    w_value,
    w_out,
):
    seq_count = lax.axis_size("seq")
    ch_count = lax.axis_size("ch")
    ch_bits = ch_count.bit_length() - 1
    me = lax.axis_index("ch")
    table = embed_table.astype(jnp.float32)
    base_in = jnp.where(masked == 1, 4, tokens)
    comp = jnp.where(masked == 1, 4, 3 - tokens)
    rev_here = jnp.flip(mirror(hidden_reverse, "seq", seq_count), axis=1)
    comp_back = jnp.flip(mirror(comp, "seq", seq_count), axis=1)
    local_width = hidden_forward.shape[-1]
    width = local_width * ch_count
    taps = conv_kernel.shape[0]
    half_width = taps // 2

    def conv_rows(hidden, bases, kernel):
        x = hidden.astype(jnp.float32) + embedded(bases, table)
        square = lax.psum(jnp.sum(x * x, axis=-1), "ch")
        normed = (x * lax.rsqrt(square[..., None] / width + 1e-05) * norm_gain).astype(jnp.bfloat16)
        length = normed.shape[1]
        padded = padded_2(normed, "seq", 1, half_width).astype(jnp.float32)
        conv = jnp.zeros(normed.shape, jnp.float32) + conv_bias
        for offset in range(taps):
            conv = conv + kernel[offset] * padded[:, offset : offset + length]
        return (x, conv.astype(jnp.bfloat16).reshape(-1, local_width))

    def activation(rows):
        pieces = gather_blocks(rows, ch_bits, me)
        dims = (((0, 2), (0, 1)), ((), ()))
        gate = lax.dot_general(
            pieces,
            w_gate.reshape(ch_count, local_width, -1),
            dims,
            preferred_element_type=jnp.float32,
        )
        value = lax.dot_general(
            pieces,
            w_value.reshape(ch_count, local_width, -1),
            dims,
            preferred_element_type=jnp.float32,
        )
        return (jax.nn.silu(gate) * value).astype(jnp.bfloat16)

    x_fwd, rows_fwd = conv_rows(hidden_forward, base_in, conv_kernel)
    _, rows_rev = conv_rows(rev_here, comp, conv_kernel[::-1])
    act_fwd = activation(rows_fwd)
    act_rev = activation(rows_rev)
    contract = (((0,), (1,)), ((), ()))
    part = lax.dot_general(w_out, act_fwd, contract, preferred_element_type=jnp.float32) + jnp.flip(
        lax.dot_general(w_out, act_rev, contract, preferred_element_type=jnp.float32), axis=0
    )
    share = scatter_blocks(part.reshape(ch_count, local_width, -1), ch_bits, me)
    out_forward = x_fwd + share.T.reshape(x_fwd.shape)
    sent = mirror(
        jnp.flip(share, axis=0).T.astype(jnp.bfloat16).reshape(x_fwd.shape),
        ("seq", "ch"),
        seq_count * ch_count,
    )
    x_rev = hidden_reverse.astype(jnp.float32) + embedded(comp_back, table)
    out_reverse = x_rev + jnp.flip(sent, axis=1).astype(jnp.float32)
    return (out_forward.astype(jnp.bfloat16), out_reverse.astype(jnp.bfloat16))


def solution(mesh):
    placed = (
        P(None, "seq"),
        P(None, "seq"),
        P(None, "seq", "ch"),
        P(None, "seq", "ch"),
        P(None, "ch"),
        P(None, "ch"),
        P("ch"),
        P("ch"),
        P(None, "ch"),
        P(None, "ch"),
        P("ch", None),
    )
    return jax.shard_map(
        local,
        mesh=mesh,
        in_specs=placed,
        out_specs=(P(None, "seq", "ch"), P(None, "seq", "ch")),
        check_vma=False,
    )
```

profile of v0, /device:TPU:17, one launch (start us, length us, event | category | flops | bytes accessed | tf_op | source)
XLA Modules:
  0.0 223.8 jit_solution(16020101666498695574)
XLA Ops:
  0.6 0.0 copy-start
  0.7 1.2 collective-permute-start.4
  1.8 1.0 fusion.34
  2.8 0.9 fusion.35
  3.7 0.7 broadcast_compare_fusion.7
  4.4 21.5 %collective-permute-done.4 = bf16[2,512,256]{2,1,0:T(8,128)(2,1)S(1)} collective-permute-done((bf16[2,512,256]{2,1,0:T(8,128)(2,1)}, bf16[2,512,256]{2,1,0:T(8,128)(2,1)S(1)}, u32[]{:S(2)}, u32[]{:S(2)}) %collective-permute-start.4) | collective-permute-done | bytes 524320 | tf_op jit(solution)/shard_map/ppermute | solution.py:8
  25.9 0.6 rev.20
  26.5 5.0 %multiply_reduce_fusion.1 = (f32[2,512]{1,0:T(2,128)S(1)}, f32[2,512]{1,0:T(2,128)S(1)}) fusion(f32[256]{0:T(256)S(1)} %bitcast.182, pred[2,512]{1,0:T(4,128)(4,1)S(1)} %get-tuple-element.51, f32[256]{0:T(256)S(1)} %bitcast.178, pred[2,512]{1,0:T(4,128)(4,1)S(1)} %get-tuple-element.53, f32[256]{0:T(256)S(1)} %bitcast.174, ...), kind=kLoop, calls=%fused_computation.67 | loop fusion | flops 6813696 | bytes 1072128 | tf_op jit(solution)/shard_map/reduce_sum | solution.py:91
  31.5 6.6 %all-reduce = (f32[2,512]{1,0:T(2,128)S(1)}, f32[2,512]{1,0:T(2,128)S(1)}) all-reduce(f32[2,512]{1,0:T(2,128)S(1)} %get-tuple-element.3, f32[2,512]{1,0:T(2,128)S(1)} %get-tuple-element.2), channel_id=1, replica_groups=mesh['seq'=8,'ch'=4] {'ch'}, use_global_device_ids=true, to_apply=%region_3.4 | all-reduce | flops 2048 | bytes 16384 | tf_op jit(solution)/shard_map/psum | solution.py:91
  38.2 1.1 multiply_convert_fusion
  39.3 3.0 %collective-permute-start.6 = (bf16[2,3,256]{2,1,0:T(4,128)(2,1)S(1)}, bf16[2,3,256]{2,1,0:T(4,128)(2,1)S(1)}, u32[]{:S(2)}, u32[]{:S(2)}) collective-permute-start(bf16[2,3,256]{2,1,0:T(4,128)(2,1)S(1)} %get-tuple-element.21), channel_id=1, source_target_pairs={{4,0},{8,4},{12,8},{16,12},{20,16},{24,20},{28,24},{5,1},{9,5},{13... | collective-permute-start | bytes 9224 | tf_op jit(solution)/shard_map/ppermute | solution.py:25
  42.4 2.3 %collective-permute-start.5 = (bf16[2,3,256]{2,1,0:T(4,128)(2,1)S(1)}, bf16[2,3,256]{2,1,0:T(4,128)(2,1)S(1)}, u32[]{:S(2)}, u32[]{:S(2)}) collective-permute-start(bf16[2,3,256]{2,1,0:T(4,128)(2,1)S(1)} %get-tuple-element.20), channel_id=1, source_target_pairs={{0,4},{4,8},{8,12},{12,16},{16,20},{20,24},{24,28},{1,5},{5,9},{9,... | collective-permute-start | bytes 9224 | tf_op jit(solution)/shard_map/ppermute | solution.py:23
  44.7 2.9 %collective-permute-done.5 = bf16[2,3,256]{2,1,0:T(4,128)(2,1)S(1)} collective-permute-done((bf16[2,3,256]{2,1,0:T(4,128)(2,1)S(1)}, bf16[2,3,256]{2,1,0:T(4,128)(2,1)S(1)}, u32[]{:S(2)}, u32[]{:S(2)}) %collective-permute-start.5) | collective-permute-done | bytes 3104 | tf_op jit(solution)/shard_map/ppermute | solution.py:23
  47.6 0.1 maximum_convert_fusion.1
  47.7 0.0 copy-start.7
  47.7 0.9 fusion.12
  48.7 1.3 collective-permute-start.7
  50.0 1.1 multiply_convert_fusion.1
  51.1 1.9 collective-permute-start.1
  53.1 3.4 %collective-permute-start = (bf16[2,3,256]{2,1,0:T(4,128)(2,1)S(1)}, bf16[2,3,256]{2,1,0:T(4,128)(2,1)S(1)}, u32[]{:S(2)}, u32[]{:S(2)}) collective-permute-start(bf16[2,3,256]{2,1,0:T(4,128)(2,1)S(1)} %get-tuple-element.18), channel_id=1, source_target_pairs={{0,4},{4,8},{8,12},{12,16},{16,20},{20,24},{24,28},{1,5},{5,9},{9,... | collective-permute-start | bytes 9224 | tf_op jit(solution)/shard_map/ppermute | solution.py:23
  56.5 1.9 collective-permute-done
  58.3 0.1 maximum_convert_fusion
  58.4 1.4 collective-permute-done.7
  59.9 1.3 select_bitcast_fusion.6
  61.1 1.1 maximum_bitcast_fusion.1
  62.2 3.3 %collective-permute-start.8 = (bf16[2,1024,256]{2,1,0:T(8,128)(2,1)}, bf16[2,1024,256]{2,1,0:T(8,128)(2,1)}, u32[]{:S(2)}, u32[]{:S(2)}) collective-permute-start(bf16[2,1024,256]{2,1,0:T(8,128)(2,1)} %maximum_bitcast_fusion.1), channel_id=1, source_target_pairs={{0,1},{1,0},{2,3},{3,2},{4,5},{5,4},{6,7},{7,6},{8,9},{9,8},{10,11... | collective-permute-start | bytes 3145736 | tf_op jit(solution)/shard_map/ppermute | solution.py:13
  65.5 1.7 fusion.20
  67.2 1.3 collective-permute-start.2
  68.5 12.5 %collective-permute-done.2 = bf16[1,1024,256]{2,1,0:T(8,128)(2,1)} collective-permute-done((bf16[1,1024,256]{2,1,0:T(8,128)(2,1)}, bf16[1,1024,256]{2,1,0:T(8,128)(2,1)}, u32[]{:S(2)}, u32[]{:S(2)}) %collective-permute-start.2) | collective-permute-done | bytes 524320 | tf_op jit(solution)/shard_map/ppermute | solution.py:13
  81.0 1.3 select_bitcast_fusion.8
  82.3 0.0 copy-start.3
  82.3 0.8 copy-done.3
  83.1 1.1 maximum_bitcast_fusion
  84.2 0.9 collective-permute-start.3
  85.0 1.4 select_bitcast_fusion.2
  86.4 0.2 pad_maximum_fusion.1
  86.6 0.1 copy.14
  86.8 4.3 %fusion.37 = f32[1024,1024,1]{1,0,2:T(8,128)} fusion(bf16[4,1024,256]{2,1,0:T(8,128)(2,1)S(1)} %bitcast.162, bf16[4,256,1024]{2,1,0:T(8,128)(2,1)S(1)} %bitcast.154), kind=kOutput, calls=%fused_computation.106 | convolution fusion | flops 2147483648 | bytes 8388608 | tf_op jit(solution)/shard_map/dot_general | solution.py:103
  91.1 10.8 %convolution_bitcast_fusion = f32[1024,1024]{1,0:T(8,128)} fusion(bf16[1024,1024]{1,0:T(8,128)(2,1)} %param.21, f32[1024,1024,1]{1,0,2:T(8,128)} %fusion.37, bf16[4,1024,256]{2,1,0:T(8,128)(2,1)} %bitcast.163, bf16[4,256,1024]{2,1,0:T(8,128)(2,1)} %bitcast.200), kind=kOutput, calls=%fused_computation.15 | convolution fusion | flops 4301258752 | bytes 14680064 | tf_op jit(solution)/shard_map/dot_general | solution.py:123
  101.8 32.9 %rev.21 = f32[1024,1024]{1,0:T(8,128)} reverse(f32[1024,1024]{1,0:T(8,128)} %convolution_bitcast_fusion), dimensions={0} | reverse | bytes 8388608 | tf_op jit(solution)/shard_map/jit(_flip)/rev | solution.py:122
  134.7 1.4 select_bitcast_fusion.4
  136.1 0.2 pad_maximum_fusion
  136.3 1.3 copy-done.10
  137.6 4.4 %fusion.36 = f32[1024,1024,1]{1,0,2:T(8,128)} fusion(bf16[4,1024,256]{2,1,0:T(8,128)(2,1)S(1)} %bitcast.160, bf16[4,256,1024]{2,1,0:T(8,128)(2,1)S(1)} %bitcast.153), kind=kOutput, calls=%fused_computation.105 | convolution fusion | flops 2147483648 | bytes 8388608 | tf_op jit(solution)/shard_map/dot_general | solution.py:103
  142.0 11.9 %bitcast_add_fusion = f32[1024,1024]{1,0:T(8,128)} fusion(f32[1024,1024]{1,0:T(8,128)} %rev.21, bf16[1024,1024]{1,0:T(8,128)(2,1)} %param.21, f32[1024,1024,1]{1,0,2:T(8,128)} %fusion.36, bf16[4,1024,256]{2,1,0:T(8,128)(2,1)} %bitcast.161, bf16[4,256,1024]{2,1,0:T(8,128)(2,1)} %bitcast.201), kind=kOutput, calls=%fused_computation.7 | convolution fusion | flops 4302307328 | bytes 18874368 | tf_op jit(solution)/shard_map/dot_general | solution.py:122
  153.9 2.8 %select_bitcast_fusion = f32[2,256,1024]{2,1,0:T(8,128)S(1)} fusion(f32[2,2,256,1024]{3,2,1,0:T(8,128)} %bitcast.155, pred[]{:T(512)S(6)} %eq.81), kind=kLoop, calls=%fused_computation.22 | loop fusion | flops 524288 | bytes 6291457 | tf_op jit(solution)/shard_map/jit(_where)/select_n | solution.py:55
  156.7 0.1 collective-permute-start.9
  156.8 4.1 %collective-permute-done.9 = f32[2,256,1024]{2,1,0:T(8,128)S(1)} collective-permute-done((f32[2,256,1024]{2,1,0:T(8,128)S(1)}, f32[2,256,1024]{2,1,0:T(8,128)S(1)}, u32[]{:S(2)}, u32[]{:S(2)}) %collective-permute-start.9) | collective-permute-done | bytes 2097184 | tf_op jit(solution)/shard_map/ppermute | solution.py:13
  160.9 0.9 fusion.10
  161.8 0.1 fusion.27
  161.9 1.3 collective-permute-start.10
  163.2 12.1 %collective-permute-done.10 = bf16[1,256,1024]{2,1,0:T(8,128)(2,1)S(1)} collective-permute-done((bf16[1,256,1024]{2,1,0:T(8,128)(2,1)S(1)}, bf16[1,256,1024]{2,1,0:T(8,128)(2,1)S(1)}, u32[]{:S(2)}, u32[]{:S(2)}) %collective-permute-start.10) | collective-permute-done | bytes 524320 | tf_op jit(solution)/shard_map/ppermute | solution.py:13
  175.3 0.8 copy-done.12
  176.1 0.3 fusion.29
  176.4 0.7 rev.23
  177.1 0.2 copy.21
  177.3 1.7 collective-permute-start.12
  179.0 2.6 %collective-permute-start.11 = (s32[2,512]{1,0:T(2,128)S(1)}, s32[2,512]{1,0:T(2,128)S(1)}, u32[]{:S(2)}, u32[]{:S(2)}) collective-permute-start(s32[2,512]{1,0:T(2,128)S(1)} %get-tuple-element.7), channel_id=1, source_target_pairs={{0,28},{4,24},{8,20},{12,16},{16,12},{20,8},{24,4},{28,0},{1,29},{... | collective-permute-start | bytes 12296 | tf_op jit(solution)/shard_map/ppermute | solution.py:8
  181.6 23.6 %collective-permute-done.11 = s32[2,512]{1,0:T(2,128)S(1)} collective-permute-done((s32[2,512]{1,0:T(2,128)S(1)}, s32[2,512]{1,0:T(2,128)S(1)}, u32[]{:S(2)}, u32[]{:S(2)}) %collective-permute-start.11) | collective-permute-done | bytes 4128 | tf_op jit(solution)/shard_map/ppermute | solution.py:8
  205.1 0.4 rev.22
  205.5 3.0 %fusion.28 = f32[1024,256]{0,1:T(8,128)} fusion(bf16[1,256,1024]{2,1,0:T(8,128)(2,1)} %copy-done.12, f32[1,2,256,1024]{3,2,1,0:T(8,128)} %copy-done.1, pred[]{:T(512)S(6)} %eq.80), kind=kLoop, calls=%fused_computation.77 | loop fusion | flops 786432 | bytes 3670017 | tf_op jit(solution)/shard_map/transpose | solution.py:126
  208.5 2.6 %copy.20 = f32[1024,256]{1,0:T(8,128)} copy(f32[1024,256]{0,1:T(8,128)} %fusion.28) | data formatting | bytes 2097152 | tf_op jit(solution)/shard_map/transpose | solution.py:126
  211.1 6.3 %rev.24 = bf16[2,512,256]{2,1,0:T(8,128)(2,1)S(1)} reverse(bf16[2,512,256]{2,1,0:T(8,128)(2,1)} %collective-permute-done.12), dimensions={1} | reverse | bytes 1048576 | tf_op jit(solution)/shard_map/jit(_flip)/rev | solution.py:133
  217.5 6.3 %add_convert_fusion = (bf16[2,512,256]{2,1,0:T(8,128)(2,1)}, bf16[2,512,256]{2,1,0:T(8,128)(2,1)}) fusion(bf16[2,512,256]{2,1,0:T(8,128)(2,1)S(1)} %rev.24, bf16[2,512,256]{2,1,0:T(8,128)(2,1)} %param.14, f32[256]{0:T(256)S(1)} %bitcast.185, f32[256]{0:T(256)S(1)} %bitcast.181, f32[256]{0:T(256)S(1)} %bitcast.177, f32[256]{0:T(256)S(1)} %bitcast.173, ...), kind=kLoop, calls=%fused_computation.56 | loop fusion | flops 7077888 | bytes 3685376 | tf_op jit(solution)/shard_map/convert_element_type | solution.py:134
  (35 shorter events, 0.1 us)
Async XLA Ops:
  0.6 86.1 %copy-start = (bf16[1024,1024]{1,0:T(8,128)(2,1)S(1)}, bf16[1024,1024]{1,0:T(8,128)(2,1)}, u32[]{:S(2)}) copy-start(bf16[1024,1024]{1,0:T(8,128)(2,1)} %param.19) | copy-start | bytes 6291460
  0.6 37.5 %copy-start.14 = (f32[256]{0:T(256)S(1)}, f32[256]{0:T(256)}, u32[]{:S(2)}) copy-start(f32[256]{0:T(256)} %param.18) | copy-start | bytes 3076
  0.7 25.2 %collective-permute-start.4 = (bf16[2,512,256]{2,1,0:T(8,128)(2,1)}, bf16[2,512,256]{2,1,0:T(8,128)(2,1)S(1)}, u32[]{:S(2)}, u32[]{:S(2)}) collective-permute-start(bf16[2,512,256]{2,1,0:T(8,128)(2,1)} %param.14), channel_id=1, source_target_pairs={{0,28},{4,24},{8,20},{12,16},{16,12},{20,8},{24,4},{28,0},{1,29},{... | collective-permute-start | bytes 1572872 | tf_op jit(solution)/shard_map/ppermute | solution.py:8
  26.5 21.2 %copy-start.13 = (f32[256]{0:T(256)S(1)}, f32[256]{0:T(256)}, u32[]{:S(2)}) copy-start(f32[256]{0:T(256)} %param.17) | copy-start | bytes 3076
  39.3 5.3 %collective-permute-start.6 = (bf16[2,3,256]{2,1,0:T(4,128)(2,1)S(1)}, bf16[2,3,256]{2,1,0:T(4,128)(2,1)S(1)}, u32[]{:S(2)}, u32[]{:S(2)}) collective-permute-start(bf16[2,3,256]{2,1,0:T(4,128)(2,1)S(1)} %get-tuple-element.21), channel_id=1, source_target_pairs={{4,0},{8,4},{12,8},{16,12},{20,16},{24,20},{28,24},{5,1},{9,5},{13... | collective-permute-start | bytes 9224 | tf_op jit(solution)/shard_map/ppermute | solution.py:25
  42.4 5.3 %collective-permute-start.5 = (bf16[2,3,256]{2,1,0:T(4,128)(2,1)S(1)}, bf16[2,3,256]{2,1,0:T(4,128)(2,1)S(1)}, u32[]{:S(2)}, u32[]{:S(2)}) collective-permute-start(bf16[2,3,256]{2,1,0:T(4,128)(2,1)S(1)} %get-tuple-element.20), channel_id=1, source_target_pairs={{0,4},{4,8},{8,12},{12,16},{16,20},{20,24},{24,28},{1,5},{5,9},{9,... | collective-permute-start | bytes 9224 | tf_op jit(solution)/shard_map/ppermute | solution.py:23
  47.7 2.3 %copy-start.7 = (bf16[2,512,256]{2,1,0:T(8,128)(2,1)S(1)}, bf16[2,512,256]{2,1,0:T(8,128)(2,1)}, u32[]{:S(2)}) copy-start(bf16[2,512,256]{2,1,0:T(8,128)(2,1)} %param.13) | copy-start | bytes 1572868
  48.7 11.2 %copy-start.9 = (bf16[2,512,256]{2,1,0:T(8,128)(2,1)}, bf16[2,512,256]{2,1,0:T(8,128)(2,1)S(1)}, u32[]{:S(2)}) copy-start(bf16[2,512,256]{2,1,0:T(8,128)(2,1)S(1)} %fusion.12) | copy-start | bytes 1572868
  48.7 11.2 %collective-permute-start.7 = (bf16[1,1024,256]{2,1,0:T(8,128)(2,1)S(1)}, bf16[1,1024,256]{2,1,0:T(8,128)(2,1)}, u32[]{:S(2)}, u32[]{:S(2)}) collective-permute-start(bf16[1,1024,256]{2,1,0:T(8,128)(2,1)S(1)} %bitcast.158), channel_id=1, source_target_pairs={{0,2},{1,3},{2,0},{3,1},{4,6},{5,7},{6,4},{7,5},{8,10},{9,11},{10,... | collective-permute-start | bytes 1572872 | tf_op jit(solution)/shard_map/ppermute | solution.py:13
  51.1 5.3 %collective-permute-start.1 = (bf16[2,3,256]{2,1,0:T(4,128)(2,1)S(1)}, bf16[2,3,256]{2,1,0:T(4,128)(2,1)S(1)}, u32[]{:S(2)}, u32[]{:S(2)}) collective-permute-start(bf16[2,3,256]{2,1,0:T(4,128)(2,1)S(1)} %get-tuple-element.19), channel_id=1, source_target_pairs={{4,0},{8,4},{12,8},{16,12},{20,16},{24,20},{28,24},{5,1},{9,5},{13... | collective-permute-start | bytes 9224 | tf_op jit(solution)/shard_map/ppermute | solution.py:25
  53.1 5.3 %collective-permute-start = (bf16[2,3,256]{2,1,0:T(4,128)(2,1)S(1)}, bf16[2,3,256]{2,1,0:T(4,128)(2,1)S(1)}, u32[]{:S(2)}, u32[]{:S(2)}) collective-permute-start(bf16[2,3,256]{2,1,0:T(4,128)(2,1)S(1)} %get-tuple-element.18), channel_id=1, source_target_pairs={{0,4},{4,8},{8,12},{12,16},{16,20},{20,24},{24,28},{1,5},{5,9},{9,... | collective-permute-start | bytes 9224 | tf_op jit(solution)/shard_map/ppermute | solution.py:23
  62.2 22.8 %collective-permute-start.8 = (bf16[2,1024,256]{2,1,0:T(8,128)(2,1)}, bf16[2,1024,256]{2,1,0:T(8,128)(2,1)}, u32[]{:S(2)}, u32[]{:S(2)}) collective-permute-start(bf16[2,1024,256]{2,1,0:T(8,128)(2,1)} %maximum_bitcast_fusion.1), channel_id=1, source_target_pairs={{0,1},{1,0},{2,3},{3,2},{4,5},{5,4},{6,7},{7,6},{8,9},{9,8},{10,11... | collective-permute-start | bytes 3145736 | tf_op jit(solution)/shard_map/ppermute | solution.py:13
  67.2 13.8 %collective-permute-start.2 = (bf16[1,1024,256]{2,1,0:T(8,128)(2,1)}, bf16[1,1024,256]{2,1,0:T(8,128)(2,1)}, u32[]{:S(2)}, u32[]{:S(2)}) collective-permute-start(bf16[1,1024,256]{2,1,0:T(8,128)(2,1)} %bitcast.12), channel_id=1, source_target_pairs={{0,2},{1,3},{2,0},{3,1},{4,6},{5,7},{6,4},{7,5},{8,10},{9,11},{10,... | collective-permute-start | bytes 1572872 | tf_op jit(solution)/shard_map/ppermute | solution.py:13
  82.3 0.8 copy-start.3
  82.3 1.9 copy-start.5
  84.2 50.5 %collective-permute-start.3 = (bf16[2,1024,256]{2,1,0:T(8,128)(2,1)}, bf16[2,1024,256]{2,1,0:T(8,128)(2,1)}, u32[]{:S(2)}, u32[]{:S(2)}) collective-permute-start(bf16[2,1024,256]{2,1,0:T(8,128)(2,1)} %maximum_bitcast_fusion), channel_id=1, source_target_pairs={{0,1},{1,0},{2,3},{3,2},{4,5},{5,4},{6,7},{7,6},{8,9},{9,8},{10,11... | collective-permute-start | bytes 3145736 | tf_op jit(solution)/shard_map/ppermute | solution.py:13
  86.7 4.3 %copy-start.11 = (bf16[2,2,1024,256]{3,2,1,0:T(8,128)(2,1)}, bf16[2,2,1024,256]{3,2,1,0:T(8,128)(2,1)S(1)}, u32[]{:S(2)}) copy-start(bf16[2,2,1024,256]{3,2,1,0:T(8,128)(2,1)S(1)} %copy.14) | copy-start | bytes 6291460
  101.8 32.9 %copy-start.4 = (bf16[1,1,1024,256]{3,2,1,0:T(8,128)(2,1)S(1)}, bf16[1,1,1024,256]{3,2,1,0:T(8,128)(2,1)}, u32[]{:S(2)}) copy-start(bf16[1,1,1024,256]{3,2,1,0:T(8,128)(2,1)} %copy-done.3) | copy-start | bytes 1572868
  101.8 32.9 %copy-start.6 = (bf16[1,1,1024,256]{3,2,1,0:T(8,128)(2,1)S(1)}, bf16[1,1,1024,256]{3,2,1,0:T(8,128)(2,1)}, u32[]{:S(2)}) copy-start(bf16[1,1,1024,256]{3,2,1,0:T(8,128)(2,1)} %copy-done.5) | copy-start | bytes 1572868
  136.3 1.4 copy-start.10
  153.9 7.0 %copy-start.2 = (f32[1024,1024]{1,0:T(8,128)S(1)}, f32[1024,1024]{1,0:T(8,128)}, u32[]{:S(2)}) copy-start(f32[1024,1024]{1,0:T(8,128)} %bitcast_add_fusion) | copy-start | bytes 12582916
  156.7 4.2 %collective-permute-start.9 = (f32[2,256,1024]{2,1,0:T(8,128)S(1)}, f32[2,256,1024]{2,1,0:T(8,128)S(1)}, u32[]{:S(2)}, u32[]{:S(2)}) collective-permute-start(f32[2,256,1024]{2,1,0:T(8,128)S(1)} %select_bitcast_fusion), channel_id=1, source_target_pairs={{0,1},{1,0},{2,3},{3,2},{4,5},{5,4},{6,7},{7,6},{8,9},{9,8},{10,11... | collective-permute-start | bytes 6291464 | tf_op jit(solution)/shard_map/ppermute | solution.py:13
  161.8 13.5 %copy-start.1 = (f32[1,2,256,1024]{3,2,1,0:T(8,128)}, f32[1,2,256,1024]{3,2,1,0:T(8,128)S(1)}, u32[]{:S(2)}) copy-start(f32[1,2,256,1024]{3,2,1,0:T(8,128)S(1)} %fusion.10) | copy-start | bytes 6291460
  161.9 13.4 %collective-permute-start.10 = (bf16[1,256,1024]{2,1,0:T(8,128)(2,1)S(1)}, bf16[1,256,1024]{2,1,0:T(8,128)(2,1)S(1)}, u32[]{:S(2)}, u32[]{:S(2)}) collective-permute-start(bf16[1,256,1024]{2,1,0:T(8,128)(2,1)S(1)} %fusion.27), channel_id=1, source_target_pairs={{0,2},{1,3},{2,0},{3,1},{4,6},{5,7},{6,4},{7,5},{8,10},{9,11},{10,... | collective-permute-start | bytes 1572872 | tf_op jit(solution)/shard_map/ppermute | solution.py:13
  175.3 0.8 copy-start.12
  177.3 33.8 %collective-permute-start.12 = (bf16[2,512,256]{2,1,0:T(8,128)(2,1)S(1)}, bf16[2,512,256]{2,1,0:T(8,128)(2,1)}, u32[]{:S(2)}, u32[]{:S(2)}) collective-permute-start(bf16[2,512,256]{2,1,0:T(8,128)(2,1)S(1)} %bitcast.165), channel_id=1, source_target_pairs={{0,31},{1,30},{2,29},{3,28},{4,27},{5,26},{6,25},{7,24},{8,23},{9,... | collective-permute-start | bytes 1572872 | tf_op jit(solution)/shard_map/ppermute | solution.py:8
  179.0 26.2 %collective-permute-start.11 = (s32[2,512]{1,0:T(2,128)S(1)}, s32[2,512]{1,0:T(2,128)S(1)}, u32[]{:S(2)}, u32[]{:S(2)}) collective-permute-start(s32[2,512]{1,0:T(2,128)S(1)} %get-tuple-element.7), channel_id=1, source_target_pairs={{0,28},{4,24},{8,20},{12,16},{16,12},{20,8},{24,4},{28,0},{1,29},{... | collective-permute-start | bytes 12296 | tf_op jit(solution)/shard_map/ppermute | solution.py:8
  208.5 9.0 %copy-start.8 = (bf16[2,512,256]{2,1,0:T(8,128)(2,1)S(1)}, bf16[2,512,256]{2,1,0:T(8,128)(2,1)}, u32[]{:S(2)}) copy-start(bf16[2,512,256]{2,1,0:T(8,128)(2,1)} %param.13) | copy-start | bytes 1572868
where the time goes:
time: 227 us; the launch traced here: 224 us
  waiting for transfers between devices  80.1 us (35%)
  local copies, waits for them, and re-layouts  48.6 us (21%)
  other arithmetic  32 us (14%)
  matrix products  31.3 us (14%)
  starting transfers between devices  24.1 us (11%)
  blocking collectives  6.62 us (3%)
    ppermute x3, waiting for transfers between devices, mirror(): return lax.ppermute(value, axes, [(k, count - 1 - k) for k in range(count)])  45 us
    rev x1, local copies, waits for them, and re-layouts, local(): jnp.flip(lax.dot_general(w_out, act_rev, contract, preferred_element_type...  32.9 us
    ppermute x6, waiting for transfers between devices, partner(): lax.ppermute(value, axis, [(k, k ^ mask) for k in range(lax.axis_size(axi...  30.2 us
    dot_general x1, matrix products, local(): lax.dot_general(w_out, act_fwd, contract, preferred_element_type=jnp.floa...  11.9 us
    dot_general x1, matrix products, local(): lax.dot_general(w_out, act_rev, contract, preferred_element_type=jnp.floa...  10.8 us
    dot_general x2, matrix products, activation(): lax.dot_general(pieces, w_gate.reshape(ch_count, local_width, -1), dims,...  8.68 us
    ppermute x6, starting transfers between devices, partner(): lax.ppermute(value, axis, [(k, k ^ mask) for k in range(lax.axis_size(axi...  8.14 us
    psum x1, blocking collectives, conv_rows(): square = lax.psum(jnp.sum(x * x, axis=-1), 'ch')  6.62 us
  transfers between devices with their start and end apart: 13, of which 8 were waited for; matrix products, arithmetic and copies ran while one was open for 28% of the time, Pallas kernels for 0%

commit v1 on v0

--- a/solution.py
+++ b/solution.py
@@ -88,7 +88,7 @@
 
     def conv_rows(hidden, bases, kernel):
         x = hidden.astype(jnp.float32) + embedded(bases, table)
-        square = lax.psum(jnp.sum(x * x, axis=-1), "ch")
+        square = jnp.sum(lax.all_gather(jnp.sum(x * x, axis=-1), "ch"), axis=0)
         normed = (x * lax.rsqrt(square[..., None] / width + 1e-05) * norm_gain).astype(jnp.bfloat16)
         length = normed.shape[1]
         padded = padded_2(normed, "seq", 1, half_width).astype(jnp.float32)

time: 227 us -> 231 us (1.018)
  blocking collectives: 6.62 us -> 12.3 us
    all_gather x0 -> x2, blocking collectives: none -> 12.3 us  [conv_rows(): square = jnp.sum(lax.all_gather(jnp.sum(x * x, axis=-1), 'ch'), axis=0)]
    psum x1 -> x0, blocking collectives: 6.62 us -> none  [conv_rows(): square = lax.psum(jnp.sum(x * x, axis=-1), 'ch')]
    ppermute x6, starting transfers between devices: 8.14 us -> 5.81 us  [partner(): lax.ppermute(value, axis, [(k, k ^ mask) for k in range(lax.axis_size(axi...]
    reduce_sum x1 -> x3, other arithmetic: 5.01 us -> 5.04 us  [conv_rows(): square = jnp.sum(lax.all_gather(jnp.sum(x * x, axis=-1), 'ch'), axis=0)]
  transfers between devices with their start and end apart: 13 -> 13, of which waited for: 8 -> 7; matrix products, arithmetic and copies ran while one was open for 28% -> 28% of each run, Pallas kernels for 0% -> 0%
where the time goes in v1:
time: 231 us; the launch traced here: 227 us
  waiting for transfers between devices  78.9 us (34%)
  local copies, waits for them, and re-layouts  48.7 us (21%)
  other arithmetic  32 us (14%)
  matrix products  31.4 us (14%)
  starting transfers between devices  22.5 us (10%)
  blocking collectives  12.3 us (5%)
    ppermute x3, waiting for transfers between devices, mirror(): return lax.ppermute(value, axes, [(k, count - 1 - k) for k in range(count)])  45.2 us
    rev x1, local copies, waits for them, and re-layouts, local(): jnp.flip(lax.dot_general(w_out, act_rev, contract, preferred_element_type...  32.9 us
    ppermute x6, waiting for transfers between devices, partner(): lax.ppermute(value, axis, [(k, k ^ mask) for k in range(lax.axis_size(axi...  30.6 us
    all_gather x2, blocking collectives, conv_rows(): square = jnp.sum(lax.all_gather(jnp.sum(x * x, axis=-1), 'ch'), axis=0)  12.3 us
    dot_general x1, matrix products, local(): lax.dot_general(w_out, act_fwd, contract, preferred_element_type=jnp.floa...  11.9 us
    dot_general x1, matrix products, local(): lax.dot_general(w_out, act_rev, contract, preferred_element_type=jnp.floa...  10.8 us
    dot_general x2, matrix products, activation(): lax.dot_general(pieces, w_gate.reshape(ch_count, local_width, -1), dims,...  8.69 us
    ppermute x2, starting transfers between devices, padded_2(): lax.ppermute(head, axis, [((i + 1) % count, i) for i in range(ends)])  6.91 us
  transfers between devices with their start and end apart: 13, of which 7 were waited for; matrix products, arithmetic and copies ran while one was open for 28% of the time, Pallas kernels for 0%

profile of v1, /device:TPU:17, one launch (start us, length us, event | category | flops | bytes accessed | tf_op | source)
XLA Modules:
  0.0 226.8 jit_solution(3446599192133551814)
XLA Ops:
  0.6 0.0 copy-start
  0.7 1.2 collective-permute-start.4
  1.8 1.0 fusion.34
  2.8 0.9 fusion.35
  3.7 0.7 broadcast_compare_fusion.7
  4.4 21.5 %collective-permute-done.4 = bf16[2,512,256]{2,1,0:T(8,128)(2,1)S(1)} collective-permute-done((bf16[2,512,256]{2,1,0:T(8,128)(2,1)}, bf16[2,512,256]{2,1,0:T(8,128)(2,1)S(1)}, u32[]{:S(2)}, u32[]{:S(2)}) %collective-permute-start.4) | collective-permute-done | bytes 524320 | tf_op jit(solution)/shard_map/ppermute | solution.py:8
  25.9 0.6 rev.20
  26.5 5.0 %multiply_reduce_fusion.1 = (f32[2,512]{1,0:T(2,128)S(1)}, f32[2,512]{1,0:T(2,128)S(1)}) fusion(f32[256]{0:T(256)S(1)} %bitcast.184, pred[2,512]{1,0:T(4,128)(4,1)S(1)} %get-tuple-element.49, f32[256]{0:T(256)S(1)} %bitcast.180, pred[2,512]{1,0:T(4,128)(4,1)S(1)} %get-tuple-element.51, f32[256]{0:T(256)S(1)} %bitcast.176, ...), kind=kLoop, calls=%fused_computation.67 | loop fusion | flops 6813696 | bytes 1072128 | tf_op jit(solution)/shard_map/reduce_sum | solution.py:91
  31.5 6.6 %all-gather.3 = f32[4,2,512]{2,1,0:T(2,128)S(1)} all-gather(f32[1,2,512]{2,1,0:T(2,128)S(1)} %bitcast.189), channel_id=3, replica_groups=mesh['seq'=8,'ch'=4] {'ch'}, dimensions={0}, use_global_device_ids=true | all-gather | bytes 20480 | tf_op jit(solution)/shard_map/all_gather | solution.py:91
  38.1 1.1 multiply_convert_fusion
  39.3 3.0 %collective-permute-start.6 = (bf16[2,3,256]{2,1,0:T(4,128)(2,1)S(1)}, bf16[2,3,256]{2,1,0:T(4,128)(2,1)S(1)}, u32[]{:S(2)}, u32[]{:S(2)}) collective-permute-start(bf16[2,3,256]{2,1,0:T(4,128)(2,1)S(1)} %get-tuple-element.19), channel_id=1, source_target_pairs={{4,0},{8,4},{12,8},{16,12},{20,16},{24,20},{28,24},{5,1},{9,5},{13... | collective-permute-start | bytes 9224 | tf_op jit(solution)/shard_map/ppermute | solution.py:25
  42.3 2.3 %collective-permute-start.5 = (bf16[2,3,256]{2,1,0:T(4,128)(2,1)S(1)}, bf16[2,3,256]{2,1,0:T(4,128)(2,1)S(1)}, u32[]{:S(2)}, u32[]{:S(2)}) collective-permute-start(bf16[2,3,256]{2,1,0:T(4,128)(2,1)S(1)} %get-tuple-element.18), channel_id=1, source_target_pairs={{0,4},{4,8},{8,12},{12,16},{16,20},{20,24},{24,28},{1,5},{5,9},{9,... | collective-permute-start | bytes 9224 | tf_op jit(solution)/shard_map/ppermute | solution.py:23
  44.6 5.8 %all-gather.2 = f32[4,2,512]{2,1,0:T(2,128)S(1)} all-gather(f32[1,2,512]{2,1,0:T(2,128)S(1)} %bitcast.188), channel_id=2, replica_groups=mesh['seq'=8,'ch'=4] {'ch'}, dimensions={0}, use_global_device_ids=true | all-gather | bytes 20480 | tf_op jit(solution)/shard_map/all_gather | solution.py:91
  50.4 0.1 maximum_convert_fusion.1
  50.6 0.0 copy-start.7
  50.6 0.9 fusion.12
  51.5 0.0 copy-start.9
  51.5 1.3 collective-permute-start.7
  52.8 1.1 multiply_convert_fusion.1
  53.9 3.9 %collective-permute-start.1 = (bf16[2,3,256]{2,1,0:T(4,128)(2,1)S(1)}, bf16[2,3,256]{2,1,0:T(4,128)(2,1)S(1)}, u32[]{:S(2)}, u32[]{:S(2)}) collective-permute-start(bf16[2,3,256]{2,1,0:T(4,128)(2,1)S(1)} %get-tuple-element.17), channel_id=1, source_target_pairs={{4,0},{8,4},{12,8},{16,12},{20,16},{24,20},{28,24},{5,1},{9,5},{13... | collective-permute-start | bytes 9224 | tf_op jit(solution)/shard_map/ppermute | solution.py:25
  57.9 2.0 collective-permute-start
  59.9 3.2 %collective-permute-done = bf16[2,3,256]{2,1,0:T(4,128)(2,1)S(1)} collective-permute-done((bf16[2,3,256]{2,1,0:T(4,128)(2,1)S(1)}, bf16[2,3,256]{2,1,0:T(4,128)(2,1)S(1)}, u32[]{:S(2)}, u32[]{:S(2)}) %collective-permute-start) | collective-permute-done | bytes 3104 | tf_op jit(solution)/shard_map/ppermute | solution.py:23
  63.1 0.1 maximum_convert_fusion
  63.2 1.7 collective-permute-done.7
  65.0 1.3 select_bitcast_fusion.6
  66.2 1.1 maximum_bitcast_fusion.1
  67.3 1.0 collective-permute-start.8
  68.4 1.7 fusion.20
  70.1 1.2 collective-permute-start.2
  71.3 12.6 %collective-permute-done.2 = bf16[1,1024,256]{2,1,0:T(8,128)(2,1)} collective-permute-done((bf16[1,1024,256]{2,1,0:T(8,128)(2,1)}, bf16[1,1024,256]{2,1,0:T(8,128)(2,1)}, u32[]{:S(2)}, u32[]{:S(2)}) %collective-permute-start.2) | collective-permute-done | bytes 524320 | tf_op jit(solution)/shard_map/ppermute | solution.py:13
  83.8 1.3 select_bitcast_fusion.8
  85.1 0.8 copy-done.3
  85.9 1.1 maximum_bitcast_fusion
  87.0 0.9 collective-permute-start.3
  87.8 1.4 select_bitcast_fusion.2
  89.2 0.2 pad_maximum_fusion.1
  89.4 0.1 copy.23
  89.6 4.3 %fusion.37 = f32[1024,1024,1]{1,0,2:T(8,128)} fusion(bf16[4,1024,256]{2,1,0:T(8,128)(2,1)S(1)} %bitcast.164, bf16[4,256,1024]{2,1,0:T(8,128)(2,1)S(1)} %bitcast.156), kind=kOutput, calls=%fused_computation.106 | convolution fusion | flops 2147483648 | bytes 8388608 | tf_op jit(solution)/shard_map/dot_general | solution.py:103
  93.9 10.8 %convolution_bitcast_fusion = f32[1024,1024]{1,0:T(8,128)} fusion(bf16[1024,1024]{1,0:T(8,128)(2,1)} %param.21, f32[1024,1024,1]{1,0,2:T(8,128)} %fusion.37, bf16[4,1024,256]{2,1,0:T(8,128)(2,1)} %bitcast.165, bf16[4,256,1024]{2,1,0:T(8,128)(2,1)} %bitcast.204), kind=kOutput, calls=%fused_computation.15 | convolution fusion | flops 4301258752 | bytes 14680064 | tf_op jit(solution)/shard_map/dot_general | solution.py:123
  104.7 32.9 %rev.21 = f32[1024,1024]{1,0:T(8,128)} reverse(f32[1024,1024]{1,0:T(8,128)} %convolution_bitcast_fusion), dimensions={0} | reverse | bytes 8388608 | tf_op jit(solution)/shard_map/jit(_flip)/rev | solution.py:122
  137.6 1.4 select_bitcast_fusion.4
  139.0 0.2 pad_maximum_fusion
  139.2 1.4 copy-done.10
  140.5 4.4 %fusion.36 = f32[1024,1024,1]{1,0,2:T(8,128)} fusion(bf16[4,1024,256]{2,1,0:T(8,128)(2,1)S(1)} %bitcast.162, bf16[4,256,1024]{2,1,0:T(8,128)(2,1)S(1)} %bitcast.155), kind=kOutput, calls=%fused_computation.105 | convolution fusion | flops 2147483648 | bytes 8388608 | tf_op jit(solution)/shard_map/dot_general | solution.py:103
  144.9 11.9 %bitcast_add_fusion = f32[1024,1024]{1,0:T(8,128)} fusion(f32[1024,1024]{1,0:T(8,128)} %rev.21, bf16[1024,1024]{1,0:T(8,128)(2,1)} %param.21, f32[1024,1024,1]{1,0,2:T(8,128)} %fusion.36, bf16[4,1024,256]{2,1,0:T(8,128)(2,1)} %bitcast.163, bf16[4,256,1024]{2,1,0:T(8,128)(2,1)} %bitcast.205), kind=kOutput, calls=%fused_computation.7 | convolution fusion | flops 4302307328 | bytes 18874368 | tf_op jit(solution)/shard_map/dot_general | solution.py:122
  156.8 2.8 %select_bitcast_fusion = f32[2,256,1024]{2,1,0:T(8,128)S(1)} fusion(f32[2,2,256,1024]{3,2,1,0:T(8,128)} %bitcast.157, pred[]{:T(512)S(6)} %eq.81), kind=kLoop, calls=%fused_computation.22 | loop fusion | flops 524288 | bytes 6291457 | tf_op jit(solution)/shard_map/jit(_where)/select_n | solution.py:55
  159.6 0.1 collective-permute-start.9
  159.7 4.1 %collective-permute-done.9 = f32[2,256,1024]{2,1,0:T(8,128)S(1)} collective-permute-done((f32[2,256,1024]{2,1,0:T(8,128)S(1)}, f32[2,256,1024]{2,1,0:T(8,128)S(1)}, u32[]{:S(2)}, u32[]{:S(2)}) %collective-permute-start.9) | collective-permute-done | bytes 2097184 | tf_op jit(solution)/shard_map/ppermute | solution.py:13
  163.8 0.9 fusion.10
  164.7 0.1 fusion.27
  164.8 1.3 collective-permute-start.10
  166.1 12.1 %collective-permute-done.10 = bf16[1,256,1024]{2,1,0:T(8,128)(2,1)S(1)} collective-permute-done((bf16[1,256,1024]{2,1,0:T(8,128)(2,1)S(1)}, bf16[1,256,1024]{2,1,0:T(8,128)(2,1)S(1)}, u32[]{:S(2)}, u32[]{:S(2)}) %collective-permute-start.10) | collective-permute-done | bytes 524320 | tf_op jit(solution)/shard_map/ppermute | solution.py:13
  178.2 0.8 copy-done.12
  179.0 0.3 fusion.29
  179.3 0.7 rev.23
  180.0 0.2 copy.30
  180.2 3.9 %collective-permute-start.12 = (bf16[2,512,256]{2,1,0:T(8,128)(2,1)S(1)}, bf16[2,512,256]{2,1,0:T(8,128)(2,1)}, u32[]{:S(2)}, u32[]{:S(2)}) collective-permute-start(bf16[2,512,256]{2,1,0:T(8,128)(2,1)S(1)} %bitcast.167), channel_id=1, source_target_pairs={{0,31},{1,30},{2,29},{3,28},{4,27},{5,26},{6,25},{7,24},{8,23},{9,... | collective-permute-start | bytes 1572872 | tf_op jit(solution)/shard_map/ppermute | solution.py:8
  184.1 0.4 collective-permute-start.11
  184.5 23.7 %collective-permute-done.11 = s32[2,512]{1,0:T(2,128)S(1)} collective-permute-done((s32[2,512]{1,0:T(2,128)S(1)}, s32[2,512]{1,0:T(2,128)S(1)}, u32[]{:S(2)}, u32[]{:S(2)}) %collective-permute-start.11) | collective-permute-done | bytes 4128 | tf_op jit(solution)/shard_map/ppermute | solution.py:8
  208.1 0.4 rev.22
  208.5 3.0 %fusion.28 = f32[1024,256]{0,1:T(8,128)} fusion(bf16[1,256,1024]{2,1,0:T(8,128)(2,1)} %copy-done.12, f32[1,2,256,1024]{3,2,1,0:T(8,128)} %copy-done.1, pred[]{:T(512)S(6)} %eq.80), kind=kLoop, calls=%fused_computation.77 | loop fusion | flops 786432 | bytes 3670017 | tf_op jit(solution)/shard_map/transpose | solution.py:126
  211.5 2.6 %copy.29 = f32[1024,256]{1,0:T(8,128)} copy(f32[1024,256]{0,1:T(8,128)} %fusion.28) | data formatting | bytes 2097152 | tf_op jit(solution)/shard_map/transpose | solution.py:126
  214.1 6.3 %rev.24 = bf16[2,512,256]{2,1,0:T(8,128)(2,1)S(1)} reverse(bf16[2,512,256]{2,1,0:T(8,128)(2,1)} %collective-permute-done.12), dimensions={1} | reverse | bytes 1048576 | tf_op jit(solution)/shard_map/jit(_flip)/rev | solution.py:133
  220.5 6.3 %add_convert_fusion = (bf16[2,512,256]{2,1,0:T(8,128)(2,1)}, bf16[2,512,256]{2,1,0:T(8,128)(2,1)}) fusion(bf16[2,512,256]{2,1,0:T(8,128)(2,1)S(1)} %rev.24, bf16[2,512,256]{2,1,0:T(8,128)(2,1)} %param.14, f32[256]{0:T(256)S(1)} %bitcast.187, f32[256]{0:T(256)S(1)} %bitcast.183, f32[256]{0:T(256)S(1)} %bitcast.179, f32[256]{0:T(256)S(1)} %bitcast.175, ...), kind=kLoop, calls=%fused_computation.56 | loop fusion | flops 7077888 | bytes 3685376 | tf_op jit(solution)/shard_map/convert_element_type | solution.py:134
  (38 shorter events, 0.2 us)
Async XLA Ops:
  0.6 88.9 %copy-start = (bf16[1024,1024]{1,0:T(8,128)(2,1)S(1)}, bf16[1024,1024]{1,0:T(8,128)(2,1)}, u32[]{:S(2)}) copy-start(bf16[1024,1024]{1,0:T(8,128)(2,1)} %param.19) | copy-start | bytes 6291460
  0.6 37.5 %copy-start.14 = (f32[256]{0:T(256)S(1)}, f32[256]{0:T(256)}, u32[]{:S(2)}) copy-start(f32[256]{0:T(256)} %param.18) | copy-start | bytes 3076
  0.7 25.2 %collective-permute-start.4 = (bf16[2,512,256]{2,1,0:T(8,128)(2,1)}, bf16[2,512,256]{2,1,0:T(8,128)(2,1)S(1)}, u32[]{:S(2)}, u32[]{:S(2)}) collective-permute-start(bf16[2,512,256]{2,1,0:T(8,128)(2,1)} %param.14), channel_id=1, source_target_pairs={{0,28},{4,24},{8,20},{12,16},{16,12},{20,8},{24,4},{28,0},{1,29},{... | collective-permute-start | bytes 1572872 | tf_op jit(solution)/shard_map/ppermute | solution.py:8
  26.5 24.0 %copy-start.13 = (f32[256]{0:T(256)S(1)}, f32[256]{0:T(256)}, u32[]{:S(2)}) copy-start(f32[256]{0:T(256)} %param.17) | copy-start | bytes 3076
  39.3 11.1 %collective-permute-start.6 = (bf16[2,3,256]{2,1,0:T(4,128)(2,1)S(1)}, bf16[2,3,256]{2,1,0:T(4,128)(2,1)S(1)}, u32[]{:S(2)}, u32[]{:S(2)}) collective-permute-start(bf16[2,3,256]{2,1,0:T(4,128)(2,1)S(1)} %get-tuple-element.19), channel_id=1, source_target_pairs={{4,0},{8,4},{12,8},{16,12},{20,16},{24,20},{28,24},{5,1},{9,5},{13... | collective-permute-start | bytes 9224 | tf_op jit(solution)/shard_map/ppermute | solution.py:25
  42.3 8.1 %collective-permute-start.5 = (bf16[2,3,256]{2,1,0:T(4,128)(2,1)S(1)}, bf16[2,3,256]{2,1,0:T(4,128)(2,1)S(1)}, u32[]{:S(2)}, u32[]{:S(2)}) collective-permute-start(bf16[2,3,256]{2,1,0:T(4,128)(2,1)S(1)} %get-tuple-element.18), channel_id=1, source_target_pairs={{0,4},{4,8},{8,12},{12,16},{16,20},{20,24},{24,28},{1,5},{5,9},{9,... | collective-permute-start | bytes 9224 | tf_op jit(solution)/shard_map/ppermute | solution.py:23
  50.6 2.2 copy-start.7
  51.5 13.5 %copy-start.9 = (bf16[2,512,256]{2,1,0:T(8,128)(2,1)}, bf16[2,512,256]{2,1,0:T(8,128)(2,1)S(1)}, u32[]{:S(2)}) copy-start(bf16[2,512,256]{2,1,0:T(8,128)(2,1)S(1)} %fusion.12) | copy-start | bytes 1572868
  51.5 13.5 %collective-permute-start.7 = (bf16[1,1024,256]{2,1,0:T(8,128)(2,1)S(1)}, bf16[1,1024,256]{2,1,0:T(8,128)(2,1)}, u32[]{:S(2)}, u32[]{:S(2)}) collective-permute-start(bf16[1,1024,256]{2,1,0:T(8,128)(2,1)S(1)} %bitcast.160), channel_id=1, source_target_pairs={{0,2},{1,3},{2,0},{3,1},{4,6},{5,7},{6,4},{7,5},{8,10},{9,11},{10,... | collective-permute-start | bytes 1572872 | tf_op jit(solution)/shard_map/ppermute | solution.py:13
  53.9 6.0 %collective-permute-start.1 = (bf16[2,3,256]{2,1,0:T(4,128)(2,1)S(1)}, bf16[2,3,256]{2,1,0:T(4,128)(2,1)S(1)}, u32[]{:S(2)}, u32[]{:S(2)}) collective-permute-start(bf16[2,3,256]{2,1,0:T(4,128)(2,1)S(1)} %get-tuple-element.17), channel_id=1, source_target_pairs={{4,0},{8,4},{12,8},{16,12},{20,16},{24,20},{28,24},{5,1},{9,5},{13... | collective-permute-start | bytes 9224 | tf_op jit(solution)/shard_map/ppermute | solution.py:25
  57.9 5.3 %collective-permute-start = (bf16[2,3,256]{2,1,0:T(4,128)(2,1)S(1)}, bf16[2,3,256]{2,1,0:T(4,128)(2,1)S(1)}, u32[]{:S(2)}, u32[]{:S(2)}) collective-permute-start(bf16[2,3,256]{2,1,0:T(4,128)(2,1)S(1)} %get-tuple-element.16), channel_id=1, source_target_pairs={{0,4},{4,8},{8,12},{12,16},{16,20},{20,24},{24,28},{1,5},{5,9},{9,... | collective-permute-start | bytes 9224 | tf_op jit(solution)/shard_map/ppermute | solution.py:23
  67.3 20.5 %collective-permute-start.8 = (bf16[2,1024,256]{2,1,0:T(8,128)(2,1)}, bf16[2,1024,256]{2,1,0:T(8,128)(2,1)}, u32[]{:S(2)}, u32[]{:S(2)}) collective-permute-start(bf16[2,1024,256]{2,1,0:T(8,128)(2,1)} %maximum_bitcast_fusion.1), channel_id=1, source_target_pairs={{0,1},{1,0},{2,3},{3,2},{4,5},{5,4},{6,7},{7,6},{8,9},{9,8},{10,11... | collective-permute-start | bytes 3145736 | tf_op jit(solution)/shard_map/ppermute | solution.py:13
  70.1 13.8 %collective-permute-start.2 = (bf16[1,1024,256]{2,1,0:T(8,128)(2,1)}, bf16[1,1024,256]{2,1,0:T(8,128)(2,1)}, u32[]{:S(2)}, u32[]{:S(2)}) collective-permute-start(bf16[1,1024,256]{2,1,0:T(8,128)(2,1)} %bitcast.13), channel_id=1, source_target_pairs={{0,2},{1,3},{2,0},{3,1},{4,6},{5,7},{6,4},{7,5},{8,10},{9,11},{10,... | collective-permute-start | bytes 1572872 | tf_op jit(solution)/shard_map/ppermute | solution.py:13
  85.1 0.8 copy-start.3
  85.1 1.8 copy-start.5
  87.0 50.6 %collective-permute-start.3 = (bf16[2,1024,256]{2,1,0:T(8,128)(2,1)}, bf16[2,1024,256]{2,1,0:T(8,128)(2,1)}, u32[]{:S(2)}, u32[]{:S(2)}) collective-permute-start(bf16[2,1024,256]{2,1,0:T(8,128)(2,1)} %maximum_bitcast_fusion), channel_id=1, source_target_pairs={{0,1},{1,0},{2,3},{3,2},{4,5},{5,4},{6,7},{7,6},{8,9},{9,8},{10,11... | collective-permute-start | bytes 3145736 | tf_op jit(solution)/shard_map/ppermute | solution.py:13
  89.6 4.3 %copy-start.11 = (bf16[2,2,1024,256]{3,2,1,0:T(8,128)(2,1)}, bf16[2,2,1024,256]{3,2,1,0:T(8,128)(2,1)S(1)}, u32[]{:S(2)}) copy-start(bf16[2,2,1024,256]{3,2,1,0:T(8,128)(2,1)S(1)} %copy.23) | copy-start | bytes 6291460
  104.7 32.9 %copy-start.4 = (bf16[1,1,1024,256]{3,2,1,0:T(8,128)(2,1)S(1)}, bf16[1,1,1024,256]{3,2,1,0:T(8,128)(2,1)}, u32[]{:S(2)}) copy-start(bf16[1,1,1024,256]{3,2,1,0:T(8,128)(2,1)} %copy-done.3) | copy-start | bytes 1572868
  104.7 32.9 %copy-start.6 = (bf16[1,1,1024,256]{3,2,1,0:T(8,128)(2,1)S(1)}, bf16[1,1,1024,256]{3,2,1,0:T(8,128)(2,1)}, u32[]{:S(2)}) copy-start(bf16[1,1,1024,256]{3,2,1,0:T(8,128)(2,1)} %copy-done.5) | copy-start | bytes 1572868
  139.2 1.4 copy-start.10
  156.8 7.0 %copy-start.2 = (f32[1024,1024]{1,0:T(8,128)S(1)}, f32[1024,1024]{1,0:T(8,128)}, u32[]{:S(2)}) copy-start(f32[1024,1024]{1,0:T(8,128)} %bitcast_add_fusion) | copy-start | bytes 12582916
  159.6 4.2 %collective-permute-start.9 = (f32[2,256,1024]{2,1,0:T(8,128)S(1)}, f32[2,256,1024]{2,1,0:T(8,128)S(1)}, u32[]{:S(2)}, u32[]{:S(2)}) collective-permute-start(f32[2,256,1024]{2,1,0:T(8,128)S(1)} %select_bitcast_fusion), channel_id=1, source_target_pairs={{0,1},{1,0},{2,3},{3,2},{4,5},{5,4},{6,7},{7,6},{8,9},{9,8},{10,11... | collective-permute-start | bytes 6291464 | tf_op jit(solution)/shard_map/ppermute | solution.py:13
  164.7 13.5 %copy-start.1 = (f32[1,2,256,1024]{3,2,1,0:T(8,128)}, f32[1,2,256,1024]{3,2,1,0:T(8,128)S(1)}, u32[]{:S(2)}) copy-start(f32[1,2,256,1024]{3,2,1,0:T(8,128)S(1)} %fusion.10) | copy-start | bytes 6291460
  164.8 13.4 %collective-permute-start.10 = (bf16[1,256,1024]{2,1,0:T(8,128)(2,1)S(1)}, bf16[1,256,1024]{2,1,0:T(8,128)(2,1)S(1)}, u32[]{:S(2)}, u32[]{:S(2)}) collective-permute-start(bf16[1,256,1024]{2,1,0:T(8,128)(2,1)S(1)} %fusion.27), channel_id=1, source_target_pairs={{0,2},{1,3},{2,0},{3,1},{4,6},{5,7},{6,4},{7,5},{8,10},{9,11},{10,... | collective-permute-start | bytes 1572872 | tf_op jit(solution)/shard_map/ppermute | solution.py:13
  178.2 0.8 copy-start.12
  180.2 33.9 %collective-permute-start.12 = (bf16[2,512,256]{2,1,0:T(8,128)(2,1)S(1)}, bf16[2,512,256]{2,1,0:T(8,128)(2,1)}, u32[]{:S(2)}, u32[]{:S(2)}) collective-permute-start(bf16[2,512,256]{2,1,0:T(8,128)(2,1)S(1)} %bitcast.167), channel_id=1, source_target_pairs={{0,31},{1,30},{2,29},{3,28},{4,27},{5,26},{6,25},{7,24},{8,23},{9,... | collective-permute-start | bytes 1572872 | tf_op jit(solution)/shard_map/ppermute | solution.py:8
  184.1 24.1 %collective-permute-start.11 = (s32[2,512]{1,0:T(2,128)S(1)}, s32[2,512]{1,0:T(2,128)S(1)}, u32[]{:S(2)}, u32[]{:S(2)}) collective-permute-start(s32[2,512]{1,0:T(2,128)S(1)} %get-tuple-element.5), channel_id=1, source_target_pairs={{0,28},{4,24},{8,20},{12,16},{16,12},{20,8},{24,4},{28,0},{1,29},{... | collective-permute-start | bytes 12296 | tf_op jit(solution)/shard_map/ppermute | solution.py:8
  211.5 9.0 %copy-start.8 = (bf16[2,512,256]{2,1,0:T(8,128)(2,1)S(1)}, bf16[2,512,256]{2,1,0:T(8,128)(2,1)}, u32[]{:S(2)}) copy-start(bf16[2,512,256]{2,1,0:T(8,128)(2,1)} %param.13) | copy-start | bytes 1572868
